TPU v7x, 32 devices: a whole 2x2x4 slice. The times are simulated.
32 devices in a mesh: rows: 8 (over z, y), sub: 4 (over x, core).
Axes of the slice: x: 2, y: 2, z: 4, core: 2. Of those that a mesh axis runs over, the one named last changes fastest.
Arguments:
- held: float32 [512, 4, 128, 256], P('rows', 'sub'), may hold values from -256 to 256
- held_block: int32 [512, 4], P('rows', 'sub'), may hold values from 0 to 255, as said below
- held_count: int32 [8, 4], P('rows', 'sub'), may hold values from 0 to 64
Outputs:
- q_factor: float32 [256, 4, 128, 256], P('rows', 'sub')
- r_factor: float32 [256, 256], replicated
Inputs may be any that keep to these rules, and one draw needn't show every extreme that they name: `held_block`: for slots j < held_count of a device, the ids are block numbers of its column group; over all devices of a column group each block is held in exactly one such slot. Slots at or past held_count hold arbitrary ids and data. A device holds at most 8 blocks whose number b has b // 32 equal to any one given device index along rows, and some device reaches that.
All inputs are finite; a program needn't handle non-finite values.
Results may differ from a plain program's by a relative error of at most 0.0003.
Values sent between devices are 32-bit elements; how exact they have to be, the bound alone decides.
No kernel may reach another device: no remote copies, remote signals or barrier semaphores. Data moves between devices by JAX's collectives and lax.ppermute only.
A program may use at most 128 MiB of HBM per device.

v0:
```python
import jax
import jax.numpy as jnp
from jax import lax
from jax.sharding import PartitionSpec as P

BLK_DEV = 32


def factor(gram):
    lower = jnp.linalg.cholesky(gram)
    identity = jnp.eye(gram.shape[0], dtype=gram.dtype)
    inverse = lax.linalg.triangular_solve(lower, identity, left_side=True, lower=True)
    return (lower, inverse)


def gram_of(flattened, total):
    return (
        lax.dot_general(
            flattened,
            flattened,
            (((0,), (0,)), ((), ())),
            precision=lax.Precision.HIGHEST,
            preferred_element_type=jnp.float32,
        )
        / total
    )


def apply_inverse(flattened, inverse):
    return jnp.dot(
        flattened, inverse.T, precision=lax.Precision.HIGHEST, preferred_element_type=jnp.float32
    )


def reduce_gram(partial_value):
    return lax.psum(partial_value, ("rows", "sub"))


def per_device(held, held_block, held_count):
    capacity = held.shape[0]
    block_rows = held.shape[2]
    width = held.shape[3]
    devices_rows = lax.axis_size("rows")
    own_index = lax.axis_index("rows")
    per_slot = max(1, capacity // devices_rows)
    total = float(devices_rows * lax.axis_size("sub") * BLK_DEV * block_rows)
    blocks = held[:, 0]
    block_ids = held_block[:, 0]
    count = held_count[0, 0]
    slots = jnp.arange(capacity, dtype=jnp.int32)
    valid = slots < count
    destination = block_ids // BLK_DEV
    earlier = (
        (destination[:, None] == destination[None, :])
        & valid[None, :]
        & (slots[None, :] < slots[:, None])
    )
    rank_within = jnp.sum(earlier.astype(jnp.int32), axis=1)
    target = jnp.where(valid, destination * per_slot + rank_within, devices_rows * per_slot)
    labels_out = block_ids.astype(jnp.float32)
    outgoing = (
        jnp.zeros((devices_rows * per_slot, block_rows, width), jnp.float32)
        .at[target]
        .set(blocks, mode="drop")
    )
    labels = (
        jnp.full((devices_rows * per_slot,), -1.0, jnp.float32)
        .at[target]
        .set(labels_out, mode="drop")
    )
    arrived = lax.all_to_all(outgoing, "rows", split_axis=0, concat_axis=0, tiled=True)
    arrived_labels = lax.all_to_all(labels, "rows", split_axis=0, concat_axis=0, tiled=True)
    local = arrived_labels.astype(jnp.int32) - own_index * BLK_DEV
    place = jnp.where(arrived_labels >= 0.0, local, BLK_DEV)
    resident = (
        jnp.zeros((BLK_DEV, block_rows, width), jnp.float32).at[place].set(arrived, mode="drop")
    )
    flattened = resident.reshape(-1, width)
    partial_one = gram_of(flattened, total)
    lower_one, inverse_one = factor(reduce_gram(partial_one))
    first = apply_inverse(flattened, inverse_one)
    lower_two, inverse_two = factor(reduce_gram(gram_of(first, total)))
    second, lower_one, lower_two = (apply_inverse(first, inverse_two), lower_one, lower_two)
    result = second.reshape(BLK_DEV, block_rows, width)
    r_factor = jnp.dot(
        lower_two.T,
        lower_one.T,
        precision=lax.Precision.HIGHEST,
        preferred_element_type=jnp.float32,
    )
    return (result[:, None], r_factor)


def solution(mesh):
    in_specs = (P("rows", "sub", None, None), P("rows", "sub"), P("rows", "sub"))
    out_specs = (P("rows", "sub", None, None), P())
    return jax.shard_map(
        per_device, mesh=mesh, in_specs=in_specs, out_specs=out_specs, check_vma=False
    )
```

profile of v0, /device:TPU:0, one launch (start us, length us, event | category | flops | bytes accessed | tf_op | source)
XLA Modules:
  0.0 661.5 jit_solution(13611043332102278474)
XLA Ops:
  7.2 0.7 bitcast_convert_fusion
  7.8 0.7 and_select_fusion
  9.3 0.8 scatter_custom_fusion
  10.1 0.7 all_to_all.9
  10.8 7.3 %all-to-all-start = ((f32[8,8,1]{1,2,0:T(1,128)}), f32[8,8,1]{1,2,0:T(1,128)S(1)}, u32[]{:S(2)}, u32[]{:S(2)}) async-start(f32[8,8,1]{1,2,0:T(1,128)} %bitcast.5), calls=%async_computation | async-start | bytes 8192 | tf_op jit(solution)/shard_map/all_to_all | solution.py:72
  18.1 4.2 broadcast_in_dim.26
  22.3 16.0 %scatter_fusion = f32[64,128,256]{2,1,0:T(8,128)} fusion(f32[64,128,256]{2,1,0:T(8,128)} %broadcast_in_dim.26, s32[64]{0:T(128)S(1)} %fusion.38, f32[64,128,256]{2,1,0:T(8,128)} %bitcast.102), kind=kCustom, calls=%fused_computation.1 | custom fusion | bytes 25166080 | tf_op jit(solution)/shard_map/scatter | solution.py:64
  38.4 5.8 all-to-all-start.1
  44.4 182.5 %all-to-all-done.1 = f32[64,128,256]{2,1,0:T(8,128)} async-done(((f32[64,128,256]{2,1,0:T(8,128)}), f32[64,128,256]{2,1,0:T(8,128)}, u32[]{:S(2)}, u32[]{:S(2)}) %all-to-all-start.1) | async-done | bytes 8388640 | tf_op jit(solution)/shard_map/all_to_all | solution.py:71
  226.9 2.5 broadcast_in_dim.11
  229.4 15.4 %scatter_fusion.1 = f32[32,128,256]{2,1,0:T(8,128)} fusion(f32[32,128,256]{2,1,0:T(8,128)} %broadcast_in_dim.11, s32[64]{0:T(128)S(1)} %fusion.37, f32[64,128,256]{2,1,0:T(8,128)} %all-to-all-done.1), kind=kCustom, calls=%fused_computation.2 | custom fusion | bytes 25166080 | tf_op jit(solution)/shard_map/scatter | solution.py:76
  244.8 10.9 %fusion = f32[256,256]{0,1:T(8,128)} fusion(f32[32,128,256]{2,1,0:T(8,128)} %scatter_fusion.1), kind=kOutput, calls=%fused_computation.9 | convolution fusion | flops 3221291008 | bytes 4456448 | tf_op jit(solution)/shard_map/dot_general | solution.py:18
  256.0 124.2 %all-reduce.4.cloned.1.call-done = f32[256,256]{0,1:T(8,128)} async-done(((f32[256,256]{0,1:T(8,128)}), f32[256,256]{0,1:T(8,128)}) %all-reduce.4.cloned.1.call-update) | async-done | bytes 262160 | tf_op jit(solution)/shard_map/psum | solution.py:36
  380.2 1.1 copy.27
  381.3 1.0 fusion.10
  382.3 11.7 %cholesky.130 = f32[128,128]{1,0:T(8,128)S(1)} custom-call(f32[128,128]{1,0:T(8,128)S(1)} %cholesky.194), custom_call_target="Cholesky" | custom-call | tf_op jit(solution)/shard_map/jit(cholesky)/cholesky | solution.py:10
  394.0 9.8 %custom-call.13 = f32[1,128,128]{1,2,0:T(8,128)S(1)} custom-call(f32[1,128,128]{2,1,0:T(8,128)S(1)} %get-tuple-element.55), custom_call_target="InvertDiagBlocksLowerTriangular" | custom-call | tf_op jit(solution)/shard_map/jit(cholesky)/cholesky | solution.py:10
  404.4 11.7 %cholesky.147 = f32[128,128]{1,0:T(8,128)S(1)} custom-call(f32[128,128]{1,0:T(8,128)S(1)} %convolution_subtract_fusion.3), custom_call_target="Cholesky" | custom-call | tf_op jit(solution)/shard_map/jit(cholesky)/cholesky | solution.py:10
  416.1 0.7 compare_reduce_fusion.2
  418.3 4.1 while.4
  418.3 0.6 fusion.63
  418.9 1.4 bitcast_dynamic-update-slice_fusion.4
  420.4 0.6 fusion.63
  421.0 1.4 bitcast_dynamic-update-slice_fusion.4
  422.4 19.7 %custom-call.14 = f32[2,128,128]{1,2,0:T(8,128)S(1)} custom-call(f32[2,128,128]{2,1,0:T(8,128)S(1)} %get-tuple-element.18), custom_call_target="InvertDiagBlocksLowerTriangular" | custom-call | tf_op jit(solution)/shard_map/triangular_solve/custom-call.0 | solution.py:12
  442.1 0.3 fusion.23
  442.7 0.3 fusion.30
  443.0 5.5 fusion.1
  448.5 1.9 copy-done
  450.4 7.4 %convolution_multiply_fusion = f32[256,256]{0,1:T(8,128)} fusion(f32[4096,256]{1,0:T(8,128)S(1)} %fusion.1), kind=kOutput, calls=%fused_computation.7 | convolution fusion | flops 3221291008 | bytes 4456448 | tf_op jit(solution)/shard_map/dot_general | solution.py:18
  457.9 124.1 %all-reduce.6.cloned.1.call-done = f32[256,256]{0,1:T(8,128)} async-done(((f32[256,256]{0,1:T(8,128)}), f32[256,256]{0,1:T(8,128)}) %all-reduce.6.cloned.1.call-update) | async-done | bytes 262160 | tf_op jit(solution)/shard_map/psum | solution.py:36
  582.0 1.1 copy.29
  583.1 1.0 fusion.9
  584.1 11.7 %cholesky.164 = f32[128,128]{1,0:T(8,128)S(1)} custom-call(f32[128,128]{1,0:T(8,128)S(1)} %cholesky.197), custom_call_target="Cholesky" | custom-call | tf_op jit(solution)/shard_map/jit(cholesky)/cholesky | solution.py:10
  595.9 10.2 %custom-call.15 = f32[1,128,128]{1,2,0:T(8,128)S(1)} custom-call(f32[1,128,128]{2,1,0:T(8,128)S(1)} %get-tuple-element.51), custom_call_target="InvertDiagBlocksLowerTriangular" | custom-call | tf_op jit(solution)/shard_map/jit(cholesky)/cholesky | solution.py:10
  606.6 11.7 %cholesky.181 = f32[128,128]{1,0:T(8,128)S(1)} custom-call(f32[128,128]{1,0:T(8,128)S(1)} %convolution_subtract_fusion.2), custom_call_target="Cholesky" | custom-call | tf_op jit(solution)/shard_map/jit(cholesky)/cholesky | solution.py:10
  618.3 0.6 compare_reduce_fusion
  619.0 0.6 compare_reduce_fusion.1
  620.9 1.2 fusion.15
  622.1 3.9 while.5
  622.2 0.6 fusion.64
  622.7 1.4 bitcast_dynamic-update-slice_fusion.5
  624.1 0.6 fusion.64
  624.7 1.4 bitcast_dynamic-update-slice_fusion.5
  626.1 19.8 %custom-call.16 = f32[2,128,128]{1,2,0:T(8,128)S(1)} custom-call(f32[2,128,128]{2,1,0:T(8,128)S(1)} %get-tuple-element.19), custom_call_target="InvertDiagBlocksLowerTriangular" | custom-call | tf_op jit(solution)/shard_map/triangular_solve/custom-call.0 | solution.py:12
  645.9 0.3 fusion.21
  646.5 0.3 fusion.26
  646.8 7.7 %fusion.5 = f32[4096,256]{1,0:T(8,128)} fusion(f32[4096,256]{1,0:T(8,128)} %copy-done, f32[128,256]{1,0:T(8,128)S(1)} %fusion.26, f32[128,256]{1,0:T(8,128)S(1)} %fusion.21), kind=kOutput, calls=%fused_computation.18 | convolution fusion | flops 3221291008 | bytes 8650752 | tf_op jit(solution)/shard_map/dot_general | solution.py:30
  (37 shorter events, 2.5 us)
Async XLA Ops:
  10.8 27.6 %all-to-all-start = ((f32[8,8,1]{1,2,0:T(1,128)}), f32[8,8,1]{1,2,0:T(1,128)S(1)}, u32[]{:S(2)}, u32[]{:S(2)}) async-start(f32[8,8,1]{1,2,0:T(1,128)} %bitcast.5), calls=%async_computation | async-start | bytes 8192 | tf_op jit(solution)/shard_map/all_to_all | solution.py:72
  38.4 188.5 %all-to-all-start.1 = ((f32[64,128,256]{2,1,0:T(8,128)}), f32[64,128,256]{2,1,0:T(8,128)}, u32[]{:S(2)}, u32[]{:S(2)}) async-start(f32[64,128,256]{2,1,0:T(8,128)} %scatter_fusion), calls=%async_computation.1 | async-start | bytes 16777216 | tf_op jit(solution)/shard_map/all_to_all | solution.py:71
  44.2 335.9 %all-reduce.4.cloned.1.call-start = ((), (), s32[]{:S(2)}) async-start(), calls=%async_computation.2 | async-start | bytes 524288 | tf_op jit(solution)/shard_map/psum | solution.py:36
  255.7 326.3 %all-reduce.6.cloned.1.call-start = ((), (), s32[]{:S(2)}) async-start(), calls=%async_computation.3 | async-start | bytes 524288 | tf_op jit(solution)/shard_map/psum | solution.py:36
  448.5 1.9 copy-start
Sparse Core Ops, SparseCore 0:
  255.8 124.3 all-reduce.3
  458.0 123.9 all-reduce.5
where the time goes:
time: 669 us; the launch traced here: 662 us
  waiting for transfers between devices  431 us (64%)
  other arithmetic  112 us (17%)
  local copies, waits for them, and re-layouts  51.9 us (8%)
  matrix products  35.4 us (5%)
  between operations  17.8 us (3%)
  starting transfers between devices  13.4 us (2%)
    psum x2, waiting for transfers between devices, reduce_gram(): return lax.psum(partial_value, ('rows', 'sub'))  248 us
    all_to_all x1, waiting for transfers between devices, per_device(): lax.all_to_all(outgoing, 'rows', split_axis=0, concat_axis=0, tiled=True)  182 us
    another operation x13, other arithmetic, factor(): lower = jnp.linalg.cholesky(gram)  69 us
    another operation x5, other arithmetic, factor(): lax.linalg.triangular_solve(lower, identity, left_side=True, lower=True)  39.6 us
    dot_general x2, matrix products, gram_of(): lax.dot_general(flattened, flattened, (((0,), (0,)), ((), ())), precision...  18.3 us
    scatter x1, local copies, waits for them, and re-layouts, per_device(): outgoing = jnp.zeros((devices_rows * per_slot, block_rows, width), jnp.fl...  16 us
    scatter x1, local copies, waits for them, and re-layouts, per_device(): jnp.zeros((BLK_DEV, block_rows, width), jnp.float32).at[place]  15.4 us
  transfers between devices with their start and end apart: 4, of which 3 were waited for; matrix products, arithmetic and copies ran while one was open for 3% of the time, Pallas kernels for 0%

commit v1 on v0

--- a/solution.py
+++ b/solution.py
@@ -4,6 +4,11 @@
 from jax.sharding import PartitionSpec as P
 
 BLK_DEV = 32
+
+
+def gather_and_add(x, axis):
+    parts = lax.all_gather(x, axis)
+    return jnp.sum(parts, axis=0)
 
 
 def factor(gram):
@@ -33,7 +38,7 @@
 
 
 def reduce_gram(partial_value):
-    return lax.psum(partial_value, ("rows", "sub"))
+    return gather_and_add(partial_value, ("rows", "sub"))
 
 
 def per_device(held, held_block, held_count):

time: 669 us -> 577 us (0.86)
  waiting for transfers between devices: 431 us -> 335 us
    psum x2 -> x0, waiting for transfers between devices: 248 us -> none  [reduce_gram(): return lax.psum(partial_value, ('rows', 'sub'))]
    all_gather x0 -> x2, waiting for transfers between devices: none -> 153 us  [gather_and_add(): parts = lax.all_gather(x, axis)]
    reduce_sum x0 -> x2, other arithmetic: none -> 7.86 us  [gather_and_add(): return jnp.sum(parts, axis=0)]
  transfers between devices with their start and end apart: 4 -> 4, of which waited for: 3 -> 3; matrix products, arithmetic and copies ran while one was open for 3% -> 4% of each run, Pallas kernels for 0% -> 0%
where the time goes in v1:
time: 577 us; the launch traced here: 570 us
  waiting for transfers between devices  335 us (58%)
  other arithmetic  118 us (20%)
  local copies, waits for them, and re-layouts  50.1 us (9%)
  matrix products  35.5 us (6%)
  between operations  17.7 us (3%)
  starting transfers between devices  13.4 us (2%)
    all_to_all x1, waiting for transfers between devices, per_device(): lax.all_to_all(outgoing, 'rows', split_axis=0, concat_axis=0, tiled=True)  182 us
    all_gather x2, waiting for transfers between devices, gather_and_add(): parts = lax.all_gather(x, axis)  153 us
    another operation x13, other arithmetic, factor(): lower = jnp.linalg.cholesky(gram)  68.9 us
    another operation x5, other arithmetic, factor(): lax.linalg.triangular_solve(lower, identity, left_side=True, lower=True)  39.6 us
    dot_general x2, matrix products, gram_of(): lax.dot_general(flattened, flattened, (((0,), (0,)), ((), ())), precision...  18.4 us
    scatter x1, local copies, waits for them, and re-layouts, per_device(): outgoing = jnp.zeros((devices_rows * per_slot, block_rows, width), jnp.fl...  16 us
    scatter x1, local copies, waits for them, and re-layouts, per_device(): jnp.zeros((BLK_DEV, block_rows, width), jnp.float32).at[place]  15.4 us
    dot_general x2, matrix products, apply_inverse(): jnp.dot(flattened, inverse.T, precision=lax.Precision.HIGHEST, preferred_...  13.2 us
  transfers between devices with their start and end apart: 4, of which 3 were waited for; matrix products, arithmetic and copies ran while one was open for 4% of the time, Pallas kernels for 0%

profile of v1, /device:TPU:0, one launch (start us, length us, event | category | flops | bytes accessed | tf_op | source)
XLA Modules:
  0.0 570.0 jit_solution(9913125497328563449)
XLA Ops:
  7.2 0.7 bitcast_convert_fusion
  7.8 0.7 and_select_fusion
  9.3 0.8 scatter_custom_fusion
  10.1 0.7 all_to_all.9
  10.8 7.3 %all-to-all-start = ((f32[8,8,1]{1,2,0:T(1,128)}), f32[8,8,1]{1,2,0:T(1,128)S(1)}, u32[]{:S(2)}, u32[]{:S(2)}) async-start(f32[8,8,1]{1,2,0:T(1,128)} %bitcast.5), calls=%async_computation | async-start | bytes 8192 | tf_op jit(solution)/shard_map/all_to_all | solution.py:77
  18.1 4.2 broadcast_in_dim.26
  22.3 16.0 %scatter_fusion = f32[64,128,256]{2,1,0:T(8,128)} fusion(f32[64,128,256]{2,1,0:T(8,128)} %broadcast_in_dim.26, s32[64]{0:T(128)S(1)} %fusion.38, f32[64,128,256]{2,1,0:T(8,128)} %bitcast.104), kind=kCustom, calls=%fused_computation.1 | custom fusion | bytes 25166080 | tf_op jit(solution)/shard_map/scatter | solution.py:69
  38.4 5.8 %all-to-all-start.1 = ((f32[64,128,256]{2,1,0:T(8,128)}), f32[64,128,256]{2,1,0:T(8,128)}, u32[]{:S(2)}, u32[]{:S(2)}) async-start(f32[64,128,256]{2,1,0:T(8,128)} %scatter_fusion), calls=%async_computation.1 | async-start | bytes 16777216 | tf_op jit(solution)/shard_map/all_to_all | solution.py:76
  44.4 182.5 %all-to-all-done.1 = f32[64,128,256]{2,1,0:T(8,128)} async-done(((f32[64,128,256]{2,1,0:T(8,128)}), f32[64,128,256]{2,1,0:T(8,128)}, u32[]{:S(2)}, u32[]{:S(2)}) %all-to-all-start.1) | async-done | bytes 8388640 | tf_op jit(solution)/shard_map/all_to_all | solution.py:76
  226.9 2.5 broadcast_in_dim.11
  229.4 15.4 %scatter_fusion.1 = f32[32,128,256]{2,1,0:T(8,128)} fusion(f32[32,128,256]{2,1,0:T(8,128)} %broadcast_in_dim.11, s32[64]{0:T(128)S(1)} %fusion.37, f32[64,128,256]{2,1,0:T(8,128)} %all-to-all-done.1), kind=kCustom, calls=%fused_computation.2 | custom fusion | bytes 25166080 | tf_op jit(solution)/shard_map/scatter | solution.py:81
  244.8 10.9 %fusion = f32[256,256]{1,0:T(8,128)} fusion(f32[32,128,256]{2,1,0:T(8,128)} %scatter_fusion.1), kind=kOutput, calls=%fused_computation.9 | convolution fusion | flops 3221291008 | bytes 4456448 | tf_op jit(solution)/shard_map/dot_general | solution.py:23
  256.0 76.6 %all-gather.5.cloned.1.call-done = f32[8192,256]{1,0:T(8,128)} async-done(((f32[256,256]{1,0:T(8,128)}), f32[8192,256]{1,0:T(8,128)}) %all-gather.5.cloned.1.call-update) | async-done | bytes 8388624 | tf_op jit(solution)/shard_map/all_gather | solution.py:10
  332.6 3.9 reduce_sum.31
  336.7 11.7 %cholesky.130 = f32[128,128]{1,0:T(8,128)S(1)} custom-call(f32[128,128]{1,0:T(8,128)S(1)} %cholesky.194), custom_call_target="Cholesky" | custom-call | tf_op jit(solution)/shard_map/jit(cholesky)/cholesky | solution.py:15
  348.5 9.8 %custom-call.13 = f32[1,128,128]{1,2,0:T(8,128)S(1)} custom-call(f32[1,128,128]{2,1,0:T(8,128)S(1)} %get-tuple-element.55), custom_call_target="InvertDiagBlocksLowerTriangular" | custom-call | tf_op jit(solution)/shard_map/jit(cholesky)/cholesky | solution.py:15
  358.5 0.3 convolution_subtract_fusion.3
  358.8 11.7 %cholesky.147 = f32[128,128]{1,0:T(8,128)S(1)} custom-call(f32[128,128]{1,0:T(8,128)S(1)} %convolution_subtract_fusion.3), custom_call_target="Cholesky" | custom-call | tf_op jit(solution)/shard_map/jit(cholesky)/cholesky | solution.py:15
  370.5 0.7 compare_reduce_fusion.2
  372.6 4.0 while.4
  372.6 0.6 fusion.63
  373.2 1.4 bitcast_dynamic-update-slice_fusion.4
  374.6 0.6 fusion.63
  375.2 1.4 bitcast_dynamic-update-slice_fusion.4
  376.6 19.7 %custom-call.14 = f32[2,128,128]{1,2,0:T(8,128)S(1)} custom-call(f32[2,128,128]{2,1,0:T(8,128)S(1)} %get-tuple-element.18), custom_call_target="InvertDiagBlocksLowerTriangular" | custom-call | tf_op jit(solution)/shard_map/triangular_solve/custom-call.0 | solution.py:17
  396.3 0.3 fusion.23
  396.8 0.3 fusion.30
  397.2 5.5 fusion.1
  402.7 2.0 copy-done
  404.6 7.5 %convolution_multiply_fusion = f32[256,256]{1,0:T(8,128)} fusion(f32[4096,256]{1,0:T(8,128)S(1)} %fusion.1), kind=kOutput, calls=%fused_computation.7 | convolution fusion | flops 3221291008 | bytes 4456448 | tf_op jit(solution)/shard_map/dot_general | solution.py:23
  412.1 76.2 %all-gather.7.cloned.1.call-done = f32[8192,256]{1,0:T(8,128)} async-done(((f32[256,256]{1,0:T(8,128)}), f32[8192,256]{1,0:T(8,128)}) %all-gather.7.cloned.1.call-update) | async-done | bytes 8388624 | tf_op jit(solution)/shard_map/all_gather | solution.py:10
  488.3 3.9 reduce_sum.32
  492.4 11.7 %cholesky.164 = f32[128,128]{1,0:T(8,128)S(1)} custom-call(f32[128,128]{1,0:T(8,128)S(1)} %cholesky.197), custom_call_target="Cholesky" | custom-call | tf_op jit(solution)/shard_map/jit(cholesky)/cholesky | solution.py:15
  504.2 10.2 %custom-call.15 = f32[1,128,128]{1,2,0:T(8,128)S(1)} custom-call(f32[1,128,128]{2,1,0:T(8,128)S(1)} %get-tuple-element.51), custom_call_target="InvertDiagBlocksLowerTriangular" | custom-call | tf_op jit(solution)/shard_map/jit(cholesky)/cholesky | solution.py:15
  514.6 0.3 convolution_subtract_fusion.2
  514.9 11.7 %cholesky.181 = f32[128,128]{1,0:T(8,128)S(1)} custom-call(f32[128,128]{1,0:T(8,128)S(1)} %convolution_subtract_fusion.2), custom_call_target="Cholesky" | custom-call | tf_op jit(solution)/shard_map/jit(cholesky)/cholesky | solution.py:15
  526.6 0.6 compare_reduce_fusion
  527.3 0.6 compare_reduce_fusion.1
  529.2 1.2 fusion.15
  530.5 4.1 while.5
  530.5 0.6 fusion.64
  531.1 1.4 bitcast_dynamic-update-slice_fusion.5
  532.5 0.6 fusion.64
  533.1 1.4 bitcast_dynamic-update-slice_fusion.5
  534.6 19.8 %custom-call.16 = f32[2,128,128]{1,2,0:T(8,128)S(1)} custom-call(f32[2,128,128]{2,1,0:T(8,128)S(1)} %get-tuple-element.19), custom_call_target="InvertDiagBlocksLowerTriangular" | custom-call | tf_op jit(solution)/shard_map/triangular_solve/custom-call.0 | solution.py:17
  554.4 0.3 fusion.21
  555.0 0.3 fusion.26
  555.3 7.7 %fusion.5 = f32[4096,256]{1,0:T(8,128)} fusion(f32[4096,256]{1,0:T(8,128)} %copy-done, f32[128,256]{1,0:T(8,128)S(1)} %fusion.26, f32[128,256]{1,0:T(8,128)S(1)} %fusion.21), kind=kOutput, calls=%fused_computation.18 | convolution fusion | flops 3221291008 | bytes 8650752 | tf_op jit(solution)/shard_map/dot_general | solution.py:35
  (39 shorter events, 2.2 us)
Async XLA Ops:
  10.8 27.6 %all-to-all-start = ((f32[8,8,1]{1,2,0:T(1,128)}), f32[8,8,1]{1,2,0:T(1,128)S(1)}, u32[]{:S(2)}, u32[]{:S(2)}) async-start(f32[8,8,1]{1,2,0:T(1,128)} %bitcast.5), calls=%async_computation | async-start | bytes 8192 | tf_op jit(solution)/shard_map/all_to_all | solution.py:77
  38.4 188.5 %all-to-all-start.1 = ((f32[64,128,256]{2,1,0:T(8,128)}), f32[64,128,256]{2,1,0:T(8,128)}, u32[]{:S(2)}, u32[]{:S(2)}) async-start(f32[64,128,256]{2,1,0:T(8,128)} %scatter_fusion), calls=%async_computation.1 | async-start | bytes 16777216 | tf_op jit(solution)/shard_map/all_to_all | solution.py:76
  44.2 288.3 %all-gather.5.cloned.1.call-start = ((), (), s32[]{:S(2)}) async-start(), calls=%async_computation.2 | async-start | bytes 8650752 | tf_op jit(solution)/shard_map/all_gather | solution.py:10
  255.7 232.6 %all-gather.7.cloned.1.call-start = ((), (), s32[]{:S(2)}) async-start(), calls=%async_computation.3 | async-start | bytes 8650752 | tf_op jit(solution)/shard_map/all_gather | solution.py:10
  402.7 2.0 copy-start
Sparse Core Ops, SparseCore 0:
  255.9 76.6 all-gather.4
  412.3 76.0 all-gather.6
